TPU v7x, 32 devices: a whole 2x2x4 slice. The times are simulated.
32 devices in a mesh: grp: 2 (over y), cell: 8 (over z, x), gene: 2 (over core).
Axes of the slice: x: 2, y: 2, z: 4, core: 2. Of those that a mesh axis runs over, the one named last changes fastest.
Arguments:
- expression: bfloat16 [2048, 16384], P(('grp', 'cell'), 'gene'), parts along dimension 0, may hold values from -6 to 6
- design: bfloat16 [2048, 128], P(('grp', 'cell')), parts along dimension 0, may hold values from -24 to 24
- quantile_level: float32 [16384], P('gene'), may hold values from 0.1 to 0.9
Outputs:
- quantile_slack: bfloat16 [2048, 16384], P(('grp', 'cell'), 'gene'), parts along dimension 0
- low_rank_coef: float32 [32768, 128], P(('grp', 'gene', 'cell')), parts along dimension 0
There are 2 independent parts, one for each index of `grp`. A program takes and returns all parts, laid end to end along the dimension named above; an argument that names none is the same for every part. Nothing has to cross between parts.
All inputs are finite; a program needn't handle non-finite values.
Results may differ from a plain program's by a relative error of at most 0.0025.
The roundings to bfloat16 on the way count: a program that leaves them out, or rounds other values in their place, can miss the bound.
Values may be sent and summed in bfloat16 or wider, within the bound.
No kernel may reach another device: no remote copies, remote signals or barrier semaphores. Data moves between devices by JAX's collectives and lax.ppermute only.
A program may use at most 64 MiB of HBM per device.

v0:
```python
import functools
import math
import jax
import jax.numpy as jnp
from jax import lax
from jax.sharding import PartitionSpec as P

NS_STEPS = 8
shrink_rate = 0.25


def matmul(left, right):
    return jnp.dot(left, right, precision=lax.Precision.HIGHEST)


def invert(matrix):
    identity = jnp.eye(matrix.shape[0], dtype=jnp.float32)
    factor = jnp.linalg.cholesky(matrix)
    lower_inv = lax.linalg.triangular_solve(factor, identity, left_side=True, lower=True)
    return matmul(lower_inv.T, lower_inv)


def newton(moment):
    identity = jnp.eye(moment.shape[0], dtype=jnp.float32)
    current = moment / jnp.trace(moment)
    root_inv = identity
    for sweep in range(NS_STEPS):
        middle = 1.5 * identity - 0.5 * matmul(root_inv, current)
        current = matmul(current, middle)
        root_inv = matmul(middle, root_inv)
    return root_inv


def cell_ring(mesh):
    devices = mesh.devices
    names = list(mesh.axis_names)
    index = [0] * len(names)
    index[names.index("cell")] = slice(None)
    line = list(devices[tuple(index)].reshape(-1))
    n = len(line)
    try:
        coords = [tuple(d.coords) for d in line]
    except (AttributeError, TypeError):
        return list(range(n))
    varying = [a for a in range(len(coords[0])) if len({c[a] for c in coords}) > 1]
    where = {c: i for i, c in enumerate(coords)}
    if len(varying) == 1:
        return sorted(range(n), key=lambda i: coords[i][varying[0]])
    if len(varying) != 2:
        return list(range(n))
    sizes = [len({c[a] for c in coords}) for a in varying]
    if sizes[0] * sizes[1] != n:
        return list(range(n))
    if sizes[0] % 2:
        varying, sizes = (varying[::-1], sizes[::-1])
        if sizes[0] % 2:
            return list(range(n))
    lows = [min((c[a] for c in coords)) for a in varying]
    path = []
    for u in range(sizes[0]):
        span = range(1, sizes[1]) if u % 2 == 0 else range(sizes[1] - 1, 0, -1)
        path += [(u, v) for v in span]
    path += [(u, 0) for u in range(sizes[0] - 1, -1, -1)]
    order = []
    for u, v in path:
        key = list(coords[0])
        key[varying[0]] = lows[0] + u
        key[varying[1]] = lows[1] + v
        order.append(where[tuple(key)])
    return order


def gather_blocks(block, axis):
    n = lax.axis_size(axis)
    me = lax.axis_index(axis)
    received = [block]
    for shift in range(1, n):
        pairs = [(i, (i + shift) % n) for i in range(n)]
        received.append(lax.ppermute(block, axis, pairs))
    stacked = jnp.stack(received)
    return jnp.take(stacked, (me - jnp.arange(n)) % n, axis=0)


def butterfly_sum(value, axis):
    n = lax.axis_size(axis)
    if n & n - 1:
        return lax.psum(value, axis)
    bit = 1
    while bit < n:
        pairs = [(i, i ^ bit) for i in range(n)]
        value = value + lax.ppermute(value, axis, pairs)
        bit *= 2
    return value


def per_device(ring, expression, design, quantile_level):
    n = len(ring)
    width = design.shape[1]
    span = expression.shape[1] // n
    identity = jnp.eye(width, dtype=jnp.float32)
    design_all = gather_blocks(design, "cell").reshape(-1, width)
    sent = expression + (design_all[0, 0] * 0).astype(expression.dtype)
    expression_genes = lax.all_to_all(sent, "cell", 1, 0, tiled=True)
    gram_total = lax.dot_general(
        design_all, design_all, (((0,), (0,)), ((), ())), preferred_element_type=jnp.float32
    )
    inverse = invert(gram_total + identity)
    crossed = lax.dot_general(
        expression_genes, design_all, (((0,), (0,)), ((), ())), preferred_element_type=jnp.float32
    )
    coef = matmul(crossed, inverse)
    local_moment = lax.dot_general(
        coef, coef, (((0,), (0,)), ((), ())), precision=lax.Precision.HIGHEST
    )
    chip_moment = butterfly_sum(local_moment, "gene")
    moment = jnp.sum(gather_blocks(chip_moment, "cell"), axis=0)
    root_inv = newton(moment)
    low_rank_coef = coef - shrink_rate / math.sqrt(width) * matmul(coef, root_inv)
    coef_low_t = coef.astype(jnp.bfloat16).T
    ring_arr = jnp.array(ring, dtype=jnp.int32)
    pos_arr = jnp.array([ring.index(i) for i in range(n)], dtype=jnp.int32)
    me = lax.axis_index("cell")
    pos = pos_arr[me]
    forward = [(ring[q], ring[(q + 1) % n]) for q in range(n)]
    backward = [(ring[(q + 1) % n], ring[q]) for q in range(n)]
    out = jnp.zeros(expression.shape, jnp.bfloat16)

    def place(out, block, owner):
        start = owner * span
        fitted = jnp.dot(design, block, preferred_element_type=jnp.float32)
        local = lax.dynamic_slice_in_dim(expression, start, span, axis=1).astype(jnp.float32)
        level = lax.dynamic_slice_in_dim(quantile_level, start, span)[None, :]
        slack = local - fitted
        piece = (slack - jnp.clip(slack, level - 1.0, level)).astype(jnp.bfloat16)
        return lax.dynamic_update_slice_in_dim(out, piece, start, axis=1)

    out = place(out, coef_low_t, me)
    ahead, behind = (coef_low_t, coef_low_t)
    for step in range(1, n // 2 + 1):
        ahead = lax.ppermute(ahead, "cell", forward)
        out = place(out, ahead, ring_arr[(pos - step) % n])
        if step <= (n - 1) // 2:
            behind = lax.ppermute(behind, "cell", backward)
            out = place(out, behind, ring_arr[(pos + step) % n])
    return (out, low_rank_coef)


def solution(mesh):
    placed = (P(("grp", "cell"), "gene"), P(("grp", "cell"), None), P("gene"))
    ring = cell_ring(mesh)
    return jax.shard_map(
        functools.partial(per_device, ring),
        mesh=mesh,
        in_specs=placed,
        out_specs=(P(("grp", "cell"), "gene"), P(("grp", "gene", "cell"), None)),
        check_vma=False,
    )
```

profile of v0, /device:TPU:0, one launch (start us, length us, event | category | flops | bytes accessed | tf_op | source)
XLA Modules:
  0.0 163.7 jit_solution(11076976861056799472)
XLA Ops:
  0.6 6.1 %collective-permute-start.6 = (bf16[128,128]{1,0:T(8,128)(2,1)}, bf16[128,128]{1,0:T(8,128)(2,1)S(1)}, u32[]{:S(2)}, u32[]{:S(2)}) collective-permute-start(bf16[128,128]{1,0:T(8,128)(2,1)} %param.6), channel_id=1, source_target_pairs={{0,14},{2,0},{4,2},{6,4},{8,6},{10,8},{12,10},{14,12},{1,15},{3,1}... | collective-permute-start | bytes 98312 | tf_op jit(solution)/shard_map/ppermute | solution.py:79
  7.1 3.0 %collective-permute-start.3 = (bf16[128,128]{1,0:T(8,128)(2,1)}, bf16[128,128]{1,0:T(8,128)(2,1)S(1)}, u32[]{:S(2)}, u32[]{:S(2)}) collective-permute-start(bf16[128,128]{1,0:T(8,128)(2,1)} %param.6), channel_id=1, source_target_pairs={{0,8},{2,10},{4,12},{6,14},{8,0},{10,2},{12,4},{14,6},{1,9},{3,11}... | collective-permute-start | bytes 98312 | tf_op jit(solution)/shard_map/ppermute | solution.py:79
  10.1 1.5 collective-permute-start
  11.7 0.8 constant_dynamic-update-slice_fusion.7
  13.1 3.2 %copy.43 = bf16[128,8192]{0,1:T(8,128)(2,1)S(1)} copy(bf16[128,8192]{1,0:T(8,128)(2,1)} %param.5) | data formatting | bytes 4194304 | tf_op args[0]
  17.0 5.7 %collective-permute-done.1 = bf16[128,128]{1,0:T(8,128)(2,1)S(1)} collective-permute-done((bf16[128,128]{1,0:T(8,128)(2,1)S(1)}, bf16[128,128]{1,0:T(8,128)(2,1)S(1)}, u32[]{:S(2)}, u32[]{:S(2)}) %collective-permute-start.1) | collective-permute-done | bytes 32800 | tf_op jit(solution)/shard_map/ppermute | solution.py:79
  22.7 5.7 %collective-permute-done.2 = bf16[128,128]{1,0:T(8,128)(2,1)S(1)} collective-permute-done((bf16[128,128]{1,0:T(8,128)(2,1)S(1)}, bf16[128,128]{1,0:T(8,128)(2,1)S(1)}, u32[]{:S(2)}, u32[]{:S(2)}) %collective-permute-start.2) | collective-permute-done | bytes 32800 | tf_op jit(solution)/shard_map/ppermute | solution.py:79
  30.9 1.5 broadcast_add_fusion
  32.4 3.9 %copy.45 = bf16[128,8,1024]{2,0,1:T(8,128)(2,1)} copy(bf16[128,8,1024]{0,2,1:T(8,128)(2,1)} %bitcast.190) | data formatting | bytes 4194304 | tf_op jit(solution)/shard_map/all_to_all | solution.py:103
  36.3 4.5 %all-to-all-start = ((bf16[128,8,1024]{2,0,1:T(8,128)(2,1)}), bf16[128,8,1024]{2,0,1:T(8,128)(2,1)}, u32[]{:S(2)}, u32[]{:S(2)}) async-start(bf16[128,8,1024]{2,0,1:T(8,128)(2,1)} %copy.45), calls=%async_computation | async-start | bytes 4194304 | tf_op jit(solution)/shard_map/all_to_all | solution.py:103
  52.4 11.7 %cholesky.29 = f32[128,128]{1,0:T(8,128)S(1)} custom-call(f32[128,128]{1,0:T(8,128)S(1)} %fusion.27), custom_call_target="Cholesky" | custom-call | tf_op jit(solution)/shard_map/jit(cholesky)/cholesky | solution.py:18
  65.5 9.8 %custom-call.6 = f32[1,128,128]{1,2,0:T(8,128)S(1)} custom-call(f32[1,128,128]{2,1,0:T(8,128)S(1)} %fusion.23), custom_call_target="InvertDiagBlocksLowerTriangular" | custom-call | tf_op jit(solution)/shard_map/triangular_solve | solution.py:19
  75.8 9.4 %all-to-all-done = bf16[128,8,1024]{2,0,1:T(8,128)(2,1)} async-done(((bf16[128,8,1024]{2,0,1:T(8,128)(2,1)}), bf16[128,8,1024]{2,0,1:T(8,128)(2,1)}, u32[]{:S(2)}, u32[]{:S(2)}) %all-to-all-start) | async-done | bytes 2097184 | tf_op jit(solution)/shard_map/all_to_all | solution.py:103
  85.2 3.9 %copy.46 = bf16[128,8,1024]{0,2,1:T(8,128)(2,1)} copy(bf16[128,8,1024]{2,0,1:T(8,128)(2,1)} %all-to-all-done) | data formatting | bytes 4194304 | tf_op jit(solution)/shard_map/all_to_all | solution.py:103
  89.1 2.4 %fusion.2 = f32[1024,128]{1,0:T(8,128)S(1)} fusion(bf16[128,8,1024]{0,2,1:T(8,128)(2,1)} %copy.46, bf16[8,128,128]{2,1,0:T(8,128)(2,1)S(1)} %gather_fusion, pred[8]{0:T(512)(128)(4,1)S(1)} %compare_and_fusion), kind=kOutput, calls=%fused_computation.4 | convolution fusion | flops 268566528 | bytes 2883592 | tf_op jit(solution)/shard_map/dot_general | solution.py:108
  92.1 1.0 fusion.38
  93.1 1.3 collective-permute-start.8
  94.4 0.8 collective-permute-start.7
  95.7 0.9 collective-permute-done.14
  96.6 1.5 bitcast_dynamic-update-slice_fusion.7
  98.1 1.3 collective-permute-start.15
  99.3 1.5 broadcast_in_dim.41
  100.9 0.7 constant_dynamic-update-slice_fusion.15
  101.6 1.4 collective-permute-start.20
  103.6 1.4 collective-permute-done.15
  106.2 4.9 %collective-permute-done.16 = f32[128,128]{1,0:T(8,128)S(1)} collective-permute-done((f32[128,128]{1,0:T(8,128)S(1)}, f32[128,128]{1,0:T(8,128)S(1)}, u32[]{:S(2)}, u32[]{:S(2)}) %collective-permute-start.16) | collective-permute-done | bytes 65568 | tf_op jit(solution)/shard_map/ppermute | solution.py:79
  112.4 4.8 %collective-permute-done.17 = f32[128,128]{1,0:T(8,128)S(1)} collective-permute-done((f32[128,128]{1,0:T(8,128)S(1)}, f32[128,128]{1,0:T(8,128)S(1)}, u32[]{:S(2)}, u32[]{:S(2)}) %collective-permute-start.17) | collective-permute-done | bytes 65568 | tf_op jit(solution)/shard_map/ppermute | solution.py:79
  117.2 1.2 collective-permute-start.18
  119.0 3.5 %collective-permute-done.18 = f32[128,128]{1,0:T(8,128)S(1)} collective-permute-done((f32[128,128]{1,0:T(8,128)S(1)}, f32[128,128]{1,0:T(8,128)S(1)}, u32[]{:S(2)}, u32[]{:S(2)}) %collective-permute-start.18) | collective-permute-done | bytes 65568 | tf_op jit(solution)/shard_map/ppermute | solution.py:79
  124.5 2.3 %collective-permute-done.21 = f32[128,128]{1,0:T(8,128)S(1)} collective-permute-done((f32[128,128]{1,0:T(8,128)S(1)}, f32[128,128]{1,0:T(8,128)S(1)}, u32[]{:S(2)}, u32[]{:S(2)}) %collective-permute-start.21) | collective-permute-done | bytes 65568 | tf_op jit(solution)/shard_map/ppermute | solution.py:79
  127.5 1.6 gather_fusion.1
  129.1 0.8 select_reduce_fusion
  130.5 0.8 fusion.21
  131.3 0.8 fusion.29
  136.6 1.4 fusion.13
  138.4 1.3 subtract_convert_fusion.6
  139.7 1.3 subtract_convert_fusion.5
  141.3 1.8 %collective-permute-start.10 = (bf16[128,1024]{0,1:T(8,128)(2,1)}, bf16[128,1024]{0,1:T(8,128)(2,1)S(1)}, u32[]{:S(2)}, u32[]{:S(2)}) collective-permute-start(bf16[128,1024]{0,1:T(8,128)(2,1)} %collective-permute-done.8), channel_id=1, source_target_pairs={{8,4},{12,8},{14,12},{10,14},{6,10},{2,6},{0,2},{4,0},{9,5},{13,9}... | collective-permute-start | bytes 786440 | tf_op jit(solution)/shard_map/ppermute | solution.py:143
  143.2 0.7 constant_dynamic-update-slice_fusion.14
  143.9 0.7 constant_dynamic-update-slice_fusion.13
  144.6 2.3 %collective-permute-done.9 = bf16[128,1024]{0,1:T(8,128)(2,1)S(1)} collective-permute-done((bf16[128,1024]{0,1:T(8,128)(2,1)}, bf16[128,1024]{0,1:T(8,128)(2,1)S(1)}, u32[]{:S(2)}, u32[]{:S(2)}) %collective-permute-start.9) | collective-permute-done | bytes 262176 | tf_op jit(solution)/shard_map/ppermute | solution.py:140
  147.5 1.5 collective-permute-done.10
  150.4 1.9 %collective-permute-start.12 = (bf16[128,1024]{0,1:T(8,128)(2,1)}, bf16[128,1024]{0,1:T(8,128)(2,1)S(1)}, u32[]{:S(2)}, u32[]{:S(2)}) collective-permute-start(bf16[128,1024]{0,1:T(8,128)(2,1)} %copy-done.7), channel_id=1, source_target_pairs={{8,4},{12,8},{14,12},{10,14},{6,10},{2,6},{0,2},{4,0},{9,5},{13,9}... | collective-permute-start | bytes 786440 | tf_op jit(solution)/shard_map/ppermute | solution.py:143
  153.0 0.7 constant_dynamic-update-slice_fusion.11
  153.7 2.4 %collective-permute-done.11 = bf16[128,1024]{0,1:T(8,128)(2,1)S(1)} collective-permute-done((bf16[128,1024]{0,1:T(8,128)(2,1)S(1)}, bf16[128,1024]{0,1:T(8,128)(2,1)S(1)}, u32[]{:S(2)}, u32[]{:S(2)}) %collective-permute-start.11) | collective-permute-done | bytes 262176 | tf_op jit(solution)/shard_map/ppermute | solution.py:140
  157.8 0.7 constant_dynamic-update-slice_fusion.10
  159.3 3.2 %collective-permute-done.13 = bf16[128,1024]{0,1:T(8,128)(2,1)S(1)} collective-permute-done((bf16[128,1024]{0,1:T(8,128)(2,1)S(1)}, bf16[128,1024]{0,1:T(8,128)(2,1)S(1)}, u32[]{:S(2)}, u32[]{:S(2)}) %collective-permute-start.13) | collective-permute-done | bytes 262176 | tf_op jit(solution)/shard_map/ppermute | solution.py:140
  163.0 0.7 constant_dynamic-update-slice_fusion.8
  (112 shorter events, 25.7 us)
Async XLA Ops:
  0.6 27.9 %collective-permute-start.6 = (bf16[128,128]{1,0:T(8,128)(2,1)}, bf16[128,128]{1,0:T(8,128)(2,1)S(1)}, u32[]{:S(2)}, u32[]{:S(2)}) collective-permute-start(bf16[128,128]{1,0:T(8,128)(2,1)} %param.6), channel_id=1, source_target_pairs={{0,14},{2,0},{4,2},{6,4},{8,6},{10,8},{12,10},{14,12},{1,15},{3,1}... | collective-permute-start | bytes 98312 | tf_op jit(solution)/shard_map/ppermute | solution.py:79
  6.7 21.8 %collective-permute-start.5 = (bf16[128,128]{1,0:T(8,128)(2,1)}, bf16[128,128]{1,0:T(8,128)(2,1)S(1)}, u32[]{:S(2)}, u32[]{:S(2)}) collective-permute-start(bf16[128,128]{1,0:T(8,128)(2,1)} %param.6), channel_id=1, source_target_pairs={{0,12},{2,14},{4,0},{6,2},{8,4},{10,6},{12,8},{14,10},{1,13},{3,15... | collective-permute-start | bytes 98312 | tf_op jit(solution)/shard_map/ppermute | solution.py:79
  7.1 21.3 %collective-permute-start.4 = (bf16[128,128]{1,0:T(8,128)(2,1)}, bf16[128,128]{1,0:T(8,128)(2,1)S(1)}, u32[]{:S(2)}, u32[]{:S(2)}) collective-permute-start(bf16[128,128]{1,0:T(8,128)(2,1)} %param.6), channel_id=1, source_target_pairs={{0,10},{2,12},{4,14},{6,0},{8,2},{10,4},{12,6},{14,8},{1,11},{3,13... | collective-permute-start | bytes 98312 | tf_op jit(solution)/shard_map/ppermute | solution.py:79
  7.1 21.3 %collective-permute-start.3 = (bf16[128,128]{1,0:T(8,128)(2,1)}, bf16[128,128]{1,0:T(8,128)(2,1)S(1)}, u32[]{:S(2)}, u32[]{:S(2)}) collective-permute-start(bf16[128,128]{1,0:T(8,128)(2,1)} %param.6), channel_id=1, source_target_pairs={{0,8},{2,10},{4,12},{6,14},{8,0},{10,2},{12,4},{14,6},{1,9},{3,11}... | collective-permute-start | bytes 98312 | tf_op jit(solution)/shard_map/ppermute | solution.py:79
  10.1 6.8 %collective-permute-start = (bf16[128,128]{1,0:T(8,128)(2,1)}, bf16[128,128]{1,0:T(8,128)(2,1)S(1)}, u32[]{:S(2)}, u32[]{:S(2)}) collective-permute-start(bf16[128,128]{1,0:T(8,128)(2,1)} %param.6), channel_id=1, source_target_pairs={{0,2},{2,4},{4,6},{6,8},{8,10},{10,12},{12,14},{14,0},{1,3},{3,5},... | collective-permute-start | bytes 98312 | tf_op jit(solution)/shard_map/ppermute | solution.py:79
  11.7 77.5 %copy-start.6 = (pred[8]{0:T(512)(128)(4,1)}, pred[8]{0:T(512)(128)(4,1)S(1)}, u32[]{:S(2)}) copy-start(pred[8]{0:T(512)(128)(4,1)S(1)} %compare_and_fusion) | copy-start | bytes 28
  13.1 3.9 %copy-start = (bf16[128,128]{1,0:T(8,128)(2,1)S(1)}, bf16[128,128]{1,0:T(8,128)(2,1)}, u32[]{:S(2)}) copy-start(bf16[128,128]{1,0:T(8,128)(2,1)} %param.6) | copy-start | bytes 98308
  17.0 5.7 %collective-permute-start.1 = (bf16[128,128]{1,0:T(8,128)(2,1)S(1)}, bf16[128,128]{1,0:T(8,128)(2,1)S(1)}, u32[]{:S(2)}, u32[]{:S(2)}) collective-permute-start(bf16[128,128]{1,0:T(8,128)(2,1)S(1)} %copy-done), channel_id=1, source_target_pairs={{0,4},{2,6},{4,8},{6,10},{8,12},{10,14},{12,0},{14,2},{1,5},{3,7},... | collective-permute-start | bytes 98312 | tf_op jit(solution)/shard_map/ppermute | solution.py:79
  22.7 5.7 %collective-permute-start.2 = (bf16[128,128]{1,0:T(8,128)(2,1)S(1)}, bf16[128,128]{1,0:T(8,128)(2,1)S(1)}, u32[]{:S(2)}, u32[]{:S(2)}) collective-permute-start(bf16[128,128]{1,0:T(8,128)(2,1)S(1)} %copy-done), channel_id=1, source_target_pairs={{0,6},{2,8},{4,10},{6,12},{8,14},{10,0},{12,2},{14,4},{1,7},{3,9},... | collective-permute-start | bytes 98312 | tf_op jit(solution)/shard_map/ppermute | solution.py:79
  36.3 4.5 %copy-start.8 = (s32[8]{0:T(128)S(1)}, s32[8]{0:T(128)}, u32[]{:S(2)}) copy-start(s32[8]{0:T(128)} %constant.188.clone) | copy-start | bytes 100
  36.3 9.8 %copy-start.2 = (s32[8]{0:T(128)S(1)}, s32[8]{0:T(128)}, u32[]{:S(2)}) copy-start(s32[8]{0:T(128)} %constant.187.clone) | copy-start | bytes 100
  36.3 15.0 %copy-start.1 = (f32[8192]{0:T(1024)S(1)}, f32[8192]{0:T(1024)}, u32[]{:S(2)}) copy-start(f32[8192]{0:T(1024)} %param.7) | copy-start | bytes 98308
  36.3 48.9 %all-to-all-start = ((bf16[128,8,1024]{2,0,1:T(8,128)(2,1)}), bf16[128,8,1024]{2,0,1:T(8,128)(2,1)}, u32[]{:S(2)}, u32[]{:S(2)}) async-start(bf16[128,8,1024]{2,0,1:T(8,128)(2,1)} %copy.45), calls=%async_computation | async-start | bytes 4194304 | tf_op jit(solution)/shard_map/all_to_all | solution.py:103
  93.1 46.6 %collective-permute-start.8 = (bf16[128,1024]{0,1:T(8,128)(2,1)S(1)}, bf16[128,1024]{0,1:T(8,128)(2,1)}, u32[]{:S(2)}, u32[]{:S(2)}) collective-permute-start(bf16[128,1024]{0,1:T(8,128)(2,1)S(1)} %convert_bitcast_fusion), channel_id=1, source_target_pairs={{8,4},{12,8},{14,12},{10,14},{6,10},{2,6},{0,2},{4,0},{9,5},{13,9}... | collective-permute-start | bytes 786440 | tf_op jit(solution)/shard_map/ppermute | solution.py:143
  94.4 43.6 %collective-permute-start.7 = (bf16[128,1024]{0,1:T(8,128)(2,1)S(1)}, bf16[128,1024]{0,1:T(8,128)(2,1)}, u32[]{:S(2)}, u32[]{:S(2)}) collective-permute-start(bf16[128,1024]{0,1:T(8,128)(2,1)S(1)} %convert_bitcast_fusion), channel_id=1, source_target_pairs={{4,8},{8,12},{12,14},{14,10},{10,6},{6,2},{2,0},{0,4},{5,9},{9,13}... | collective-permute-start | bytes 786440 | tf_op jit(solution)/shard_map/ppermute | solution.py:140
  95.2 1.4 collective-permute-start.14
  98.1 7.0 %collective-permute-start.15 = (f32[128,128]{1,0:T(8,128)S(1)}, f32[128,128]{1,0:T(8,128)S(1)}, u32[]{:S(2)}, u32[]{:S(2)}) collective-permute-start(f32[128,128]{1,0:T(8,128)S(1)} %get-tuple-element.3), channel_id=1, source_target_pairs={{0,2},{2,4},{4,6},{6,8},{8,10},{10,12},{12,14},{14,0},{1,3},{3,5},... | collective-permute-start | bytes 196616 | tf_op jit(solution)/shard_map/ppermute | solution.py:79
  101.6 22.3 %collective-permute-start.20 = (f32[128,128]{1,0:T(8,128)S(1)}, f32[128,128]{1,0:T(8,128)S(1)}, u32[]{:S(2)}, u32[]{:S(2)}) collective-permute-start(f32[128,128]{1,0:T(8,128)S(1)} %get-tuple-element.3), channel_id=1, source_target_pairs={{0,12},{2,14},{4,0},{6,2},{8,4},{10,6},{12,8},{14,10},{1,13},{3,15... | collective-permute-start | bytes 196616 | tf_op jit(solution)/shard_map/ppermute | solution.py:79
  103.0 20.2 %collective-permute-start.19 = (f32[128,128]{1,0:T(8,128)S(1)}, f32[128,128]{1,0:T(8,128)S(1)}, u32[]{:S(2)}, u32[]{:S(2)}) collective-permute-start(f32[128,128]{1,0:T(8,128)S(1)} %get-tuple-element.3), channel_id=1, source_target_pairs={{0,10},{2,12},{4,14},{6,0},{8,2},{10,4},{12,6},{14,8},{1,11},{3,13... | collective-permute-start | bytes 196616 | tf_op jit(solution)/shard_map/ppermute | solution.py:79
  105.0 6.1 %collective-permute-start.16 = (f32[128,128]{1,0:T(8,128)S(1)}, f32[128,128]{1,0:T(8,128)S(1)}, u32[]{:S(2)}, u32[]{:S(2)}) collective-permute-start(f32[128,128]{1,0:T(8,128)S(1)} %get-tuple-element.3), channel_id=1, source_target_pairs={{0,4},{2,6},{4,8},{6,10},{8,12},{10,14},{12,0},{14,2},{1,5},{3,7},... | collective-permute-start | bytes 196616 | tf_op jit(solution)/shard_map/ppermute | solution.py:79
  111.1 6.1 %collective-permute-start.17 = (f32[128,128]{1,0:T(8,128)S(1)}, f32[128,128]{1,0:T(8,128)S(1)}, u32[]{:S(2)}, u32[]{:S(2)}) collective-permute-start(f32[128,128]{1,0:T(8,128)S(1)} %get-tuple-element.3), channel_id=1, source_target_pairs={{0,6},{2,8},{4,10},{6,12},{8,14},{10,0},{12,2},{14,4},{1,7},{3,9},... | collective-permute-start | bytes 196616 | tf_op jit(solution)/shard_map/ppermute | solution.py:79
  117.2 5.4 %collective-permute-start.18 = (f32[128,128]{1,0:T(8,128)S(1)}, f32[128,128]{1,0:T(8,128)S(1)}, u32[]{:S(2)}, u32[]{:S(2)}) collective-permute-start(f32[128,128]{1,0:T(8,128)S(1)} %get-tuple-element.3), channel_id=1, source_target_pairs={{0,8},{2,10},{4,12},{6,14},{8,0},{10,2},{12,4},{14,6},{1,9},{3,11}... | collective-permute-start | bytes 196616 | tf_op jit(solution)/shard_map/ppermute | solution.py:79
  122.6 4.3 %collective-permute-start.21 = (f32[128,128]{1,0:T(8,128)S(1)}, f32[128,128]{1,0:T(8,128)S(1)}, u32[]{:S(2)}, u32[]{:S(2)}) collective-permute-start(f32[128,128]{1,0:T(8,128)S(1)} %get-tuple-element.3), channel_id=1, source_target_pairs={{0,14},{2,0},{4,2},{6,4},{8,6},{10,8},{12,10},{14,12},{1,15},{3,1}... | collective-permute-start | bytes 196616 | tf_op jit(solution)/shard_map/ppermute | solution.py:79
  133.2 5.1 %copy-start.4 = (f32[1024]{0:T(1024)S(1)}, f32[1024]{0:T(1024)}, u32[]{:S(2)}) copy-start(f32[1024]{0:T(1024)} %get-tuple-element.28) | copy-start | bytes 12292
  133.2 5.1 %copy-start.5 = (f32[1024]{0:T(1024)S(1)}, f32[1024]{0:T(1024)}, u32[]{:S(2)}) copy-start(f32[1024]{0:T(1024)} %get-tuple-element.29) | copy-start | bytes 12292
  134.3 5.4 %copy-start.3 = (f32[1024]{0:T(1024)S(1)}, f32[1024]{0:T(1024)}, u32[]{:S(2)}) copy-start(f32[1024]{0:T(1024)} %get-tuple-element.27) | copy-start | bytes 12292
  138.0 8.9 %collective-permute-start.9 = (bf16[128,1024]{0,1:T(8,128)(2,1)}, bf16[128,1024]{0,1:T(8,128)(2,1)S(1)}, u32[]{:S(2)}, u32[]{:S(2)}) collective-permute-start(bf16[128,1024]{0,1:T(8,128)(2,1)} %collective-permute-done.7), channel_id=1, source_target_pairs={{4,8},{8,12},{12,14},{14,10},{10,6},{6,2},{2,0},{0,4},{5,9},{9,13}... | collective-permute-start | bytes 786440 | tf_op jit(solution)/shard_map/ppermute | solution.py:140
  141.3 7.7 %collective-permute-start.10 = (bf16[128,1024]{0,1:T(8,128)(2,1)}, bf16[128,1024]{0,1:T(8,128)(2,1)S(1)}, u32[]{:S(2)}, u32[]{:S(2)}) collective-permute-start(bf16[128,1024]{0,1:T(8,128)(2,1)} %collective-permute-done.8), channel_id=1, source_target_pairs={{8,4},{12,8},{14,12},{10,14},{6,10},{2,6},{0,2},{4,0},{9,5},{13,9}... | collective-permute-start | bytes 786440 | tf_op jit(solution)/shard_map/ppermute | solution.py:143
  146.9 9.2 %collective-permute-start.11 = (bf16[128,1024]{0,1:T(8,128)(2,1)S(1)}, bf16[128,1024]{0,1:T(8,128)(2,1)S(1)}, u32[]{:S(2)}, u32[]{:S(2)}) collective-permute-start(bf16[128,1024]{0,1:T(8,128)(2,1)S(1)} %collective-permute-done.9), channel_id=1, source_target_pairs={{4,8},{8,12},{12,14},{14,10},{10,6},{6,2},{2,0},{0,4},{5,9},{9,13}... | collective-permute-start | bytes 786440 | tf_op jit(solution)/shard_map/ppermute | solution.py:140
  149.0 0.7 copy-start.7
  150.4 6.8 %collective-permute-start.12 = (bf16[128,1024]{0,1:T(8,128)(2,1)}, bf16[128,1024]{0,1:T(8,128)(2,1)S(1)}, u32[]{:S(2)}, u32[]{:S(2)}) collective-permute-start(bf16[128,1024]{0,1:T(8,128)(2,1)} %copy-done.7), channel_id=1, source_target_pairs={{8,4},{12,8},{14,12},{10,14},{6,10},{2,6},{0,2},{4,0},{9,5},{13,9}... | collective-permute-start | bytes 786440 | tf_op jit(solution)/shard_map/ppermute | solution.py:143
  156.1 6.4 %collective-permute-start.13 = (bf16[128,1024]{0,1:T(8,128)(2,1)S(1)}, bf16[128,1024]{0,1:T(8,128)(2,1)S(1)}, u32[]{:S(2)}, u32[]{:S(2)}) collective-permute-start(bf16[128,1024]{0,1:T(8,128)(2,1)S(1)} %collective-permute-done.11), channel_id=1, source_target_pairs={{4,8},{8,12},{12,14},{14,10},{10,6},{6,2},{2,0},{0,4},{5,9},{9,13}... | collective-permute-start | bytes 786440 | tf_op jit(solution)/shard_map/ppermute | solution.py:140
where the time goes:
time: 165 us; the launch traced here: 164 us
  waiting for transfers between devices  49.3 us (30%)
  local copies, waits for them, and re-layouts  30.2 us (18%)
  other arithmetic  27.9 us (17%)
  starting transfers between devices  27.7 us (17%)
  matrix products  16.9 us (10%)
  between operations  11.7 us (7%)
    ppermute x14, waiting for transfers between devices, gather_blocks(): received.append(lax.ppermute(block, axis, pairs))  29 us
    ppermute x14, starting transfers between devices, gather_blocks(): received.append(lax.ppermute(block, axis, pairs))  16.8 us
    another operation x3, other arithmetic, invert(): factor = jnp.linalg.cholesky(matrix)  12.4 us
    another operation x2, other arithmetic, invert(): lax.linalg.triangular_solve(factor, identity, left_side=True, lower=True)  10.5 us
    all_to_all x1, waiting for transfers between devices, per_device(): expression_genes = lax.all_to_all(sent, 'cell', 1, 0, tiled=True)  9.38 us
    unnamed x32, local copies, waits for them, and re-layouts  8.62 us
    dot_general x26, matrix products, matmul(): return jnp.dot(left, right, precision=lax.Precision.HIGHEST)  8.15 us
    ppermute x4, waiting for transfers between devices, per_device(): ahead = lax.ppermute(ahead, 'cell', forward)  7.9 us
  transfers between devices with their start and end apart: 23, of which 15 were waited for; matrix products, arithmetic and copies ran while one was open for 36% of the time, Pallas kernels for 0%

commit v1 on v0

--- a/solution.py
+++ b/solution.py
@@ -7,6 +7,38 @@
 
 NS_STEPS = 8
 shrink_rate = 0.25
+
+
+def time_indices(values, ndim_at, piece_in):
+    arr_now = values.shape
+    e_now = values.reshape(
+        *arr_now[:ndim_at], piece_in, arr_now[ndim_at] // piece_in, *arr_now[ndim_at + 1 :]
+    )
+    return jnp.moveaxis(e_now, ndim_at, 0)
+
+
+def store_object(patch, which_dim):
+    seen_now = list(patch.shape[1:])
+    seen_now[which_dim] *= patch.shape[0]
+    return jnp.moveaxis(patch, 0, which_dim).reshape(seen_now)
+
+
+def edge_open(along_axis, xs, mine, mat=1):
+    next_value = lax.axis_size(along_axis)
+    outcome_arr, u1 = (next_value, lax.axis_index(along_axis))
+    near = time_indices(xs, mat, outcome_arr)
+    stack_in = [near[u1]]
+    dd = 1
+    while dd < outcome_arr:
+        now = near[u1 ^ dd]
+        new = lax.ppermute(
+            now, axis_name=along_axis, perm=[(dev_j, dev_j ^ dd) for dev_j in range(outcome_arr)]
+        )
+        stack_in.append(new)
+        dd = dd + 1
+    z2 = jnp.stack(stack_in, 0)
+    near = z2[u1 ^ jnp.arange(outcome_arr)]
+    return store_object(near, mine)
 
 
 def matmul(left, right):
@@ -100,7 +132,7 @@
     identity = jnp.eye(width, dtype=jnp.float32)
     design_all = gather_blocks(design, "cell").reshape(-1, width)
     sent = expression + (design_all[0, 0] * 0).astype(expression.dtype)
-    expression_genes = lax.all_to_all(sent, "cell", 1, 0, tiled=True)
+    expression_genes = edge_open("cell", sent, 0)
     gram_total = lax.dot_general(
         design_all, design_all, (((0,), (0,)), ((), ())), preferred_element_type=jnp.float32
     )

time: 165 us -> 172 us (1.042)
  waiting for transfers between devices: 49.3 us -> 19.2 us
  starting transfers between devices: 27.7 us -> 49.1 us
  local copies, waits for them, and re-layouts: 30.2 us -> 47.2 us
    ppermute x14, waiting for transfers between devices: 29 us -> 8.58 us  [gather_blocks(): received.append(lax.ppermute(block, axis, pairs))]
    ppermute x0 -> x7, starting transfers between devices: none -> 11.3 us  [edge_open(): lax.ppermute(now, axis_name=along_axis, perm=[(dev_j, dev_j ^ dd) for dev...]
    another operation x0 -> x10, local copies, waits for them, and re-layouts: none -> 9.85 us
    unnamed x32 -> x47, local copies, waits for them, and re-layouts: 8.62 us -> 18.4 us
    all_to_all x1 -> x0, waiting for transfers between devices: 9.38 us -> none  [per_device(): expression_genes = lax.all_to_all(sent, 'cell', 1, 0, tiled=True)]
    ppermute x14, starting transfers between devices: 16.8 us -> 25.3 us  [gather_blocks(): received.append(lax.ppermute(block, axis, pairs))]
    all_to_all x2 -> x0, local copies, waits for them, and re-layouts: 7.81 us -> none  [per_device(): expression_genes = lax.all_to_all(sent, 'cell', 1, 0, tiled=True)]
    ppermute x4, starting transfers between devices: 1.28 us -> 8.06 us  [per_device(): ahead = lax.ppermute(ahead, 'cell', forward)]
  transfers between devices with their start and end apart: 23 -> 29, of which waited for: 15 -> 12; matrix products, arithmetic and copies ran while one was open for 36% -> 43% of each run, Pallas kernels for 0% -> 0%
where the time goes in v1:
time: 172 us; the launch traced here: 171 us
  starting transfers between devices  49.1 us (29%)
  local copies, waits for them, and re-layouts  47.2 us (27%)
  other arithmetic  26.6 us (15%)
  waiting for transfers between devices  19.2 us (11%)
  matrix products  16.9 us (10%)
  between operations  11.8 us (7%)
    ppermute x14, starting transfers between devices, gather_blocks(): received.append(lax.ppermute(block, axis, pairs))  25.3 us
    unnamed x47, local copies, waits for them, and re-layouts  18.4 us
    another operation x3, other arithmetic, invert(): factor = jnp.linalg.cholesky(matrix)  12.4 us
    ppermute x7, starting transfers between devices, edge_open(): lax.ppermute(now, axis_name=along_axis, perm=[(dev_j, dev_j ^ dd) for dev...  11.3 us
    another operation x2, other arithmetic, invert(): lax.linalg.triangular_solve(factor, identity, left_side=True, lower=True)  10.4 us
    another operation x9, local copies, waits for them, and re-layouts  9.13 us
    ppermute x14, waiting for transfers between devices, gather_blocks(): received.append(lax.ppermute(block, axis, pairs))  8.58 us
    dot_general x26, matrix products, matmul(): return jnp.dot(left, right, precision=lax.Precision.HIGHEST)  8.14 us
  transfers between devices with their start and end apart: 29, of which 12 were waited for; matrix products, arithmetic and copies ran while one was open for 43% of the time, Pallas kernels for 0%

profile of v1, /device:TPU:0, one launch (start us, length us, event | category | flops | bytes accessed | tf_op | source)
XLA Modules:
  0.0 170.8 jit_solution(10292764795907207086)
XLA Ops:
  0.6 3.0 %collective-permute-start = (bf16[128,128]{1,0:T(8,128)(2,1)}, bf16[128,128]{1,0:T(8,128)(2,1)S(1)}, u32[]{:S(2)}, u32[]{:S(2)}) collective-permute-start(bf16[128,128]{1,0:T(8,128)(2,1)} %param.6), channel_id=1, source_target_pairs={{0,2},{2,4},{4,6},{6,8},{8,10},{10,12},{12,14},{14,0},{1,3},{3,5},... | collective-permute-start | bytes 98312 | tf_op jit(solution)/shard_map/ppermute | solution.py:111
  3.6 1.6 collective-permute-start.1
  5.2 2.6 %collective-permute-start.2 = (bf16[128,128]{1,0:T(8,128)(2,1)}, bf16[128,128]{1,0:T(8,128)(2,1)S(1)}, u32[]{:S(2)}, u32[]{:S(2)}) collective-permute-start(bf16[128,128]{1,0:T(8,128)(2,1)} %param.6), channel_id=1, source_target_pairs={{0,6},{2,8},{4,10},{6,12},{8,14},{10,0},{12,2},{14,4},{1,7},{3,9},... | collective-permute-start | bytes 98312 | tf_op jit(solution)/shard_map/ppermute | solution.py:111
  7.8 1.2 collective-permute-start.3
  9.0 2.6 %collective-permute-start.4 = (bf16[128,128]{1,0:T(8,128)(2,1)}, bf16[128,128]{1,0:T(8,128)(2,1)S(1)}, u32[]{:S(2)}, u32[]{:S(2)}) collective-permute-start(bf16[128,128]{1,0:T(8,128)(2,1)} %param.6), channel_id=1, source_target_pairs={{0,10},{2,12},{4,14},{6,0},{8,2},{10,4},{12,6},{14,8},{1,11},{3,13... | collective-permute-start | bytes 98312 | tf_op jit(solution)/shard_map/ppermute | solution.py:111
  12.5 1.2 dynamic_slice.85
  18.4 1.6 fusion.31
  24.6 1.4 broadcast_add_fusion.1
  26.5 3.2 %copy.43 = bf16[128,8192]{0,1:T(8,128)(2,1)S(1)} copy(bf16[128,8192]{1,0:T(8,128)(2,1)} %param.5) | data formatting | bytes 4194304 | tf_op args[0]
  29.8 1.4 collective-permute-start.5
  31.2 1.5 collective-permute-start.6
  33.8 1.4 collective-permute-done.6
  39.1 1.8 %copy.45 = bf16[128,1,1024]{2,0,1:T(8,128)(2,1)} copy(bf16[128,1,1024]{0,2,1:T(8,128)(2,1)} %get-tuple-element.27) | data formatting | bytes 524288 | tf_op jit(solution)/shard_map/dynamic-slice
  40.9 1.7 bitcast_dynamic-update-slice_fusion.7
  42.6 1.8 %copy.46 = bf16[128,1,1024]{2,0,1:T(8,128)(2,1)} copy(bf16[128,1,1024]{0,2,1:T(8,128)(2,1)} %get-tuple-element.26) | data formatting | bytes 524288 | tf_op jit(solution)/shard_map/dynamic-slice.1
  44.3 1.5 collective-permute-start.7
  45.9 1.8 %copy.47 = bf16[128,1,1024]{2,0,1:T(8,128)(2,1)} copy(bf16[128,1,1024]{0,2,1:T(8,128)(2,1)} %get-tuple-element.25) | data formatting | bytes 524288 | tf_op jit(solution)/shard_map/dynamic-slice.2
  48.6 1.8 %collective-permute-start.9 = (bf16[128,1024]{1,0:T(8,128)(2,1)}, bf16[128,1024]{1,0:T(8,128)(2,1)}, u32[]{:S(2)}, u32[]{:S(2)}) collective-permute-start(bf16[128,1024]{1,0:T(8,128)(2,1)} %bitcast.214), channel_id=1, source_target_pairs={{0,6},{2,4},{4,2},{6,0},{8,14},{10,12},{12,10},{14,8},{1,7},{3,5},... | collective-permute-start | bytes 786440 | tf_op jit(solution)/shard_map/ppermute | solution.py:34
  51.3 1.8 %collective-permute-start.10 = (bf16[128,1024]{1,0:T(8,128)(2,1)}, bf16[128,1024]{1,0:T(8,128)(2,1)}, u32[]{:S(2)}, u32[]{:S(2)}) collective-permute-start(bf16[128,1024]{1,0:T(8,128)(2,1)} %bitcast.20), channel_id=1, source_target_pairs={{0,8},{2,10},{4,12},{6,14},{8,0},{10,2},{12,4},{14,6},{1,9},{3,11}... | collective-permute-start | bytes 786440 | tf_op jit(solution)/shard_map/ppermute | solution.py:34
  53.2 2.2 %collective-permute-start.11 = (bf16[128,1024]{1,0:T(8,128)(2,1)S(1)}, bf16[128,1024]{1,0:T(8,128)(2,1)S(1)}, u32[]{:S(2)}, u32[]{:S(2)}) collective-permute-start(bf16[128,1024]{1,0:T(8,128)(2,1)S(1)} %bitcast.213), channel_id=1, source_target_pairs={{0,10},{2,8},{4,14},{6,12},{8,2},{10,0},{12,6},{14,4},{1,11},{3,9}... | collective-permute-start | bytes 786440 | tf_op jit(solution)/shard_map/ppermute | solution.py:34
  55.6 11.7 %cholesky.29 = f32[128,128]{1,0:T(8,128)S(1)} custom-call(f32[128,128]{1,0:T(8,128)S(1)} %fusion.22), custom_call_target="Cholesky" | custom-call | tf_op jit(solution)/shard_map/jit(cholesky)/cholesky | solution.py:50
  68.5 9.8 %custom-call.6 = f32[1,128,128]{1,2,0:T(8,128)S(1)} custom-call(f32[1,128,128]{2,1,0:T(8,128)S(1)} %fusion.18), custom_call_target="InvertDiagBlocksLowerTriangular" | custom-call | tf_op jit(solution)/shard_map/triangular_solve | solution.py:51
  79.9 3.2 %collective-permute-start.12 = (bf16[128,1024]{1,0:T(8,128)(2,1)}, bf16[128,1024]{1,0:T(8,128)(2,1)S(1)}, u32[]{:S(2)}, u32[]{:S(2)}) collective-permute-start(bf16[128,1024]{1,0:T(8,128)(2,1)} %bitcast.218), channel_id=1, source_target_pairs={{0,12},{2,14},{4,8},{6,10},{8,4},{10,6},{12,0},{14,2},{1,13},{3,15... | collective-permute-start | bytes 786440 | tf_op jit(solution)/shard_map/ppermute | solution.py:34
  83.1 1.7 bitcast_dynamic-update-slice_fusion.6
  85.4 1.7 bitcast_dynamic-update-slice_fusion.5
  87.1 1.7 bitcast_dynamic-update-slice_fusion.4
  88.7 1.7 bitcast_dynamic-update-slice_fusion.3
  91.9 2.1 %collective-permute-done.13 = bf16[128,1024]{1,0:T(8,128)(2,1)S(1)} collective-permute-done((bf16[128,1024]{1,0:T(8,128)(2,1)S(1)}, bf16[128,1024]{1,0:T(8,128)(2,1)S(1)}, u32[]{:S(2)}, u32[]{:S(2)}) %collective-permute-start.13) | collective-permute-done | bytes 262176 | tf_op jit(solution)/shard_map/ppermute | solution.py:34
  94.7 3.7 %gather_fusion.1 = bf16[8,128,1024]{2,1,0:T(8,128)(2,1)} fusion(bf16[8,128,1024]{2,1,0:T(8,128)(2,1)} %bitcast_dynamic-update-slice_fusion, s32[1024]{0:T(1024)S(1)} %pad_clamp_fusion), kind=kCustom, calls=%fused_computation.1 | custom fusion | bytes 4194336 | tf_op jit(solution)/shard_map/gather | solution.py:40
  98.3 2.4 %convolution_bitcast_fusion.8 = f32[1024,128]{1,0:T(8,128)S(1)} fusion(bf16[8,128,1024]{2,1,0:T(8,128)(2,1)} %gather_fusion.1, bf16[8,128,128]{2,1,0:T(8,128)(2,1)S(1)} %copy-done.1, pred[8]{0:T(512)(128)(4,1)S(1)} %copy-done.10), kind=kOutput, calls=%fused_computation.19 | convolution fusion | flops 268566528 | bytes 2883592 | tf_op jit(solution)/shard_map/dot_general | solution.py:140
  102.4 8.1 %collective-permute-start.14 = (bf16[128,1024]{0,1:T(8,128)(2,1)S(1)}, bf16[128,1024]{0,1:T(8,128)(2,1)}, u32[]{:S(2)}, u32[]{:S(2)}) collective-permute-start(bf16[128,1024]{0,1:T(8,128)(2,1)S(1)} %convert_bitcast_fusion), channel_id=1, source_target_pairs={{4,8},{8,12},{12,14},{14,10},{10,6},{6,2},{2,0},{0,4},{5,9},{9,13}... | collective-permute-start | bytes 786440 | tf_op jit(solution)/shard_map/ppermute | solution.py:172
  111.8 1.5 bitcast_dynamic-update-slice_fusion.15
  113.3 1.7 collective-permute-start.22
  115.0 1.5 broadcast_in_dim.42
  117.2 1.8 %collective-permute-start.23 = (f32[128,128]{1,0:T(8,128)S(1)}, f32[128,128]{1,0:T(8,128)S(1)}, u32[]{:S(2)}, u32[]{:S(2)}) collective-permute-start(f32[128,128]{1,0:T(8,128)S(1)} %get-tuple-element.3), channel_id=1, source_target_pairs={{0,4},{2,6},{4,8},{6,10},{8,12},{10,14},{12,0},{14,2},{1,5},{3,7},... | collective-permute-start | bytes 196616 | tf_op jit(solution)/shard_map/ppermute | solution.py:111
  120.2 2.6 %collective-permute-start.25 = (f32[128,128]{1,0:T(8,128)S(1)}, f32[128,128]{1,0:T(8,128)S(1)}, u32[]{:S(2)}, u32[]{:S(2)}) collective-permute-start(f32[128,128]{1,0:T(8,128)S(1)} %get-tuple-element.3), channel_id=1, source_target_pairs={{0,8},{2,10},{4,12},{6,14},{8,0},{10,2},{12,4},{14,6},{1,9},{3,11}... | collective-permute-start | bytes 196616 | tf_op jit(solution)/shard_map/ppermute | solution.py:111
  125.0 3.8 %collective-permute-done.24 = f32[128,128]{1,0:T(8,128)S(1)} collective-permute-done((f32[128,128]{1,0:T(8,128)S(1)}, f32[128,128]{1,0:T(8,128)S(1)}, u32[]{:S(2)}, u32[]{:S(2)}) %collective-permute-start.24) | collective-permute-done | bytes 65568 | tf_op jit(solution)/shard_map/ppermute | solution.py:111
  128.8 3.2 %collective-permute-start.27 = (f32[128,128]{1,0:T(8,128)S(1)}, f32[128,128]{1,0:T(8,128)S(1)}, u32[]{:S(2)}, u32[]{:S(2)}) collective-permute-start(f32[128,128]{1,0:T(8,128)S(1)} %get-tuple-element.3), channel_id=1, source_target_pairs={{0,12},{2,14},{4,0},{6,2},{8,4},{10,6},{12,8},{14,10},{1,13},{3,15... | collective-permute-start | bytes 196616 | tf_op jit(solution)/shard_map/ppermute | solution.py:111
  134.7 2.2 %collective-permute-done.28 = f32[128,128]{1,0:T(8,128)S(1)} collective-permute-done((f32[128,128]{1,0:T(8,128)S(1)}, f32[128,128]{1,0:T(8,128)S(1)}, u32[]{:S(2)}, u32[]{:S(2)}) %collective-permute-start.28) | collective-permute-done | bytes 65568 | tf_op jit(solution)/shard_map/ppermute | solution.py:111
  137.5 1.6 gather_fusion.2
  146.1 1.4 fusion.8
  147.5 1.3 subtract_convert_fusion.6
  148.8 1.3 subtract_convert_fusion.5
  150.4 2.1 %collective-permute-start.17 = (bf16[128,1024]{0,1:T(8,128)(2,1)}, bf16[128,1024]{0,1:T(8,128)(2,1)S(1)}, u32[]{:S(2)}, u32[]{:S(2)}) collective-permute-start(bf16[128,1024]{0,1:T(8,128)(2,1)} %collective-permute-done.15), channel_id=1, source_target_pairs={{8,4},{12,8},{14,12},{10,14},{6,10},{2,6},{0,2},{4,0},{9,5},{13,9}... | collective-permute-start | bytes 786440 | tf_op jit(solution)/shard_map/ppermute | solution.py:175
  155.5 1.6 collective-permute-done.17
  158.4 2.4 %collective-permute-start.19 = (bf16[128,1024]{0,1:T(8,128)(2,1)}, bf16[128,1024]{0,1:T(8,128)(2,1)S(1)}, u32[]{:S(2)}, u32[]{:S(2)}) collective-permute-start(bf16[128,1024]{0,1:T(8,128)(2,1)} %copy-done.12), channel_id=1, source_target_pairs={{8,4},{12,8},{14,12},{10,14},{6,10},{2,6},{0,2},{4,0},{9,5},{13,9}... | collective-permute-start | bytes 786440 | tf_op jit(solution)/shard_map/ppermute | solution.py:175
  163.6 1.5 collective-permute-done.19
  167.2 2.4 %collective-permute-done.20 = bf16[128,1024]{0,1:T(8,128)(2,1)S(1)} collective-permute-done((bf16[128,1024]{0,1:T(8,128)(2,1)S(1)}, bf16[128,1024]{0,1:T(8,128)(2,1)S(1)}, u32[]{:S(2)}, u32[]{:S(2)}) %collective-permute-start.20) | collective-permute-done | bytes 262176 | tf_op jit(solution)/shard_map/ppermute | solution.py:172
  (150 shorter events, 40.4 us)
Async XLA Ops:
  0.6 29.2 %collective-permute-start = (bf16[128,128]{1,0:T(8,128)(2,1)}, bf16[128,128]{1,0:T(8,128)(2,1)S(1)}, u32[]{:S(2)}, u32[]{:S(2)}) collective-permute-start(bf16[128,128]{1,0:T(8,128)(2,1)} %param.6), channel_id=1, source_target_pairs={{0,2},{2,4},{4,6},{6,8},{8,10},{10,12},{12,14},{14,0},{1,3},{3,5},... | collective-permute-start | bytes 98312 | tf_op jit(solution)/shard_map/ppermute | solution.py:111
  3.6 27.6 %collective-permute-start.1 = (bf16[128,128]{1,0:T(8,128)(2,1)}, bf16[128,128]{1,0:T(8,128)(2,1)S(1)}, u32[]{:S(2)}, u32[]{:S(2)}) collective-permute-start(bf16[128,128]{1,0:T(8,128)(2,1)} %param.6), channel_id=1, source_target_pairs={{0,4},{2,6},{4,8},{6,10},{8,12},{10,14},{12,0},{14,2},{1,5},{3,7},... | collective-permute-start | bytes 98312 | tf_op jit(solution)/shard_map/ppermute | solution.py:111
  5.2 27.5 %collective-permute-start.2 = (bf16[128,128]{1,0:T(8,128)(2,1)}, bf16[128,128]{1,0:T(8,128)(2,1)S(1)}, u32[]{:S(2)}, u32[]{:S(2)}) collective-permute-start(bf16[128,128]{1,0:T(8,128)(2,1)} %param.6), channel_id=1, source_target_pairs={{0,6},{2,8},{4,10},{6,12},{8,14},{10,0},{12,2},{14,4},{1,7},{3,9},... | collective-permute-start | bytes 98312 | tf_op jit(solution)/shard_map/ppermute | solution.py:111
  7.8 25.0 %collective-permute-start.3 = (bf16[128,128]{1,0:T(8,128)(2,1)}, bf16[128,128]{1,0:T(8,128)(2,1)S(1)}, u32[]{:S(2)}, u32[]{:S(2)}) collective-permute-start(bf16[128,128]{1,0:T(8,128)(2,1)} %param.6), channel_id=1, source_target_pairs={{0,8},{2,10},{4,12},{6,14},{8,0},{10,2},{12,4},{14,6},{1,9},{3,11}... | collective-permute-start | bytes 98312 | tf_op jit(solution)/shard_map/ppermute | solution.py:111
  9.0 23.8 %collective-permute-start.4 = (bf16[128,128]{1,0:T(8,128)(2,1)}, bf16[128,128]{1,0:T(8,128)(2,1)S(1)}, u32[]{:S(2)}, u32[]{:S(2)}) collective-permute-start(bf16[128,128]{1,0:T(8,128)(2,1)} %param.6), channel_id=1, source_target_pairs={{0,10},{2,12},{4,14},{6,0},{8,2},{10,4},{12,6},{14,8},{1,11},{3,13... | collective-permute-start | bytes 98312 | tf_op jit(solution)/shard_map/ppermute | solution.py:111
  12.5 23.3 %copy-start.9 = (pred[8]{0:T(512)(128)(4,1)}, pred[8]{0:T(512)(128)(4,1)S(1)}, u32[]{:S(2)}) copy-start(pred[8]{0:T(512)(128)(4,1)S(1)} %compare_and_fusion) | copy-start | bytes 28
  26.5 3.3 %copy-start.2 = (bf16[128,128]{1,0:T(8,128)(2,1)S(1)}, bf16[128,128]{1,0:T(8,128)(2,1)}, u32[]{:S(2)}) copy-start(bf16[128,128]{1,0:T(8,128)(2,1)} %param.6) | copy-start | bytes 98308
  29.8 4.0 %collective-permute-start.5 = (bf16[128,128]{1,0:T(8,128)(2,1)S(1)}, bf16[128,128]{1,0:T(8,128)(2,1)S(1)}, u32[]{:S(2)}, u32[]{:S(2)}) collective-permute-start(bf16[128,128]{1,0:T(8,128)(2,1)S(1)} %copy-done.2), channel_id=1, source_target_pairs={{0,12},{2,14},{4,0},{6,2},{8,4},{10,6},{12,8},{14,10},{1,13},{3,15... | collective-permute-start | bytes 98312 | tf_op jit(solution)/shard_map/ppermute | solution.py:111
  31.2 4.0 %collective-permute-start.6 = (bf16[128,128]{1,0:T(8,128)(2,1)S(1)}, bf16[128,128]{1,0:T(8,128)(2,1)S(1)}, u32[]{:S(2)}, u32[]{:S(2)}) collective-permute-start(bf16[128,128]{1,0:T(8,128)(2,1)S(1)} %copy-done.2), channel_id=1, source_target_pairs={{0,14},{2,0},{4,2},{6,4},{8,6},{10,8},{12,10},{14,12},{1,15},{3,1}... | collective-permute-start | bytes 98312 | tf_op jit(solution)/shard_map/ppermute | solution.py:111
  35.8 2.3 %copy-start = (bf16[8,128,128]{2,1,0:T(8,128)(2,1)}, bf16[8,128,128]{2,1,0:T(8,128)(2,1)S(1)}, u32[]{:S(2)}) copy-start(bf16[8,128,128]{2,1,0:T(8,128)(2,1)S(1)} %gather_fusion) | copy-start | bytes 786436
  44.3 35.6 %collective-permute-start.7 = (bf16[128,1024]{1,0:T(8,128)(2,1)}, bf16[128,1024]{1,0:T(8,128)(2,1)}, u32[]{:S(2)}, u32[]{:S(2)}) collective-permute-start(bf16[128,1024]{1,0:T(8,128)(2,1)} %bitcast.216), channel_id=1, source_target_pairs={{0,2},{2,0},{4,6},{6,4},{8,10},{10,8},{12,14},{14,12},{1,3},{3,1},... | collective-permute-start | bytes 786440 | tf_op jit(solution)/shard_map/ppermute | solution.py:34
  47.7 37.1 %collective-permute-start.8 = (bf16[128,1024]{1,0:T(8,128)(2,1)}, bf16[128,1024]{1,0:T(8,128)(2,1)}, u32[]{:S(2)}, u32[]{:S(2)}) collective-permute-start(bf16[128,1024]{1,0:T(8,128)(2,1)} %bitcast.215), channel_id=1, source_target_pairs={{0,4},{2,6},{4,0},{6,2},{8,12},{10,14},{12,8},{14,10},{1,5},{3,7},... | collective-permute-start | bytes 786440 | tf_op jit(solution)/shard_map/ppermute | solution.py:34
  48.6 38.4 %collective-permute-start.9 = (bf16[128,1024]{1,0:T(8,128)(2,1)}, bf16[128,1024]{1,0:T(8,128)(2,1)}, u32[]{:S(2)}, u32[]{:S(2)}) collective-permute-start(bf16[128,1024]{1,0:T(8,128)(2,1)} %bitcast.214), channel_id=1, source_target_pairs={{0,6},{2,4},{4,2},{6,0},{8,14},{10,12},{12,10},{14,8},{1,7},{3,5},... | collective-permute-start | bytes 786440 | tf_op jit(solution)/shard_map/ppermute | solution.py:34
  51.3 37.4 %collective-permute-start.10 = (bf16[128,1024]{1,0:T(8,128)(2,1)}, bf16[128,1024]{1,0:T(8,128)(2,1)}, u32[]{:S(2)}, u32[]{:S(2)}) collective-permute-start(bf16[128,1024]{1,0:T(8,128)(2,1)} %bitcast.20), channel_id=1, source_target_pairs={{0,8},{2,10},{4,12},{6,14},{8,0},{10,2},{12,4},{14,6},{1,9},{3,11}... | collective-permute-start | bytes 786440 | tf_op jit(solution)/shard_map/ppermute | solution.py:34
  53.2 37.2 %collective-permute-start.11 = (bf16[128,1024]{1,0:T(8,128)(2,1)S(1)}, bf16[128,1024]{1,0:T(8,128)(2,1)S(1)}, u32[]{:S(2)}, u32[]{:S(2)}) collective-permute-start(bf16[128,1024]{1,0:T(8,128)(2,1)S(1)} %bitcast.213), channel_id=1, source_target_pairs={{0,10},{2,8},{4,14},{6,12},{8,2},{10,0},{12,6},{14,4},{1,11},{3,9}... | collective-permute-start | bytes 786440 | tf_op jit(solution)/shard_map/ppermute | solution.py:34
  79.9 11.2 %collective-permute-start.12 = (bf16[128,1024]{1,0:T(8,128)(2,1)}, bf16[128,1024]{1,0:T(8,128)(2,1)S(1)}, u32[]{:S(2)}, u32[]{:S(2)}) collective-permute-start(bf16[128,1024]{1,0:T(8,128)(2,1)} %bitcast.218), channel_id=1, source_target_pairs={{0,12},{2,14},{4,8},{6,10},{8,4},{10,6},{12,0},{14,2},{1,13},{3,15... | collective-permute-start | bytes 786440 | tf_op jit(solution)/shard_map/ppermute | solution.py:34
  84.8 9.1 %collective-permute-start.13 = (bf16[128,1024]{1,0:T(8,128)(2,1)S(1)}, bf16[128,1024]{1,0:T(8,128)(2,1)S(1)}, u32[]{:S(2)}, u32[]{:S(2)}) collective-permute-start(bf16[128,1024]{1,0:T(8,128)(2,1)S(1)} %bitcast.217), channel_id=1, source_target_pairs={{0,14},{2,12},{4,10},{6,8},{8,6},{10,4},{12,2},{14,0},{1,15},{3,13... | collective-permute-start | bytes 786440 | tf_op jit(solution)/shard_map/ppermute | solution.py:34
  94.7 3.7 %copy-start.1 = (bf16[8,128,128]{2,1,0:T(8,128)(2,1)S(1)}, bf16[8,128,128]{2,1,0:T(8,128)(2,1)}, u32[]{:S(2)}) copy-start(bf16[8,128,128]{2,1,0:T(8,128)(2,1)} %copy-done) | copy-start | bytes 786436
  94.7 3.7 %copy-start.10 = (pred[8]{0:T(512)(128)(4,1)S(1)}, pred[8]{0:T(512)(128)(4,1)}, u32[]{:S(2)}) copy-start(pred[8]{0:T(512)(128)(4,1)} %copy-done.9) | copy-start | bytes 28
  102.4 45.1 %collective-permute-start.14 = (bf16[128,1024]{0,1:T(8,128)(2,1)S(1)}, bf16[128,1024]{0,1:T(8,128)(2,1)}, u32[]{:S(2)}, u32[]{:S(2)}) collective-permute-start(bf16[128,1024]{0,1:T(8,128)(2,1)S(1)} %convert_bitcast_fusion), channel_id=1, source_target_pairs={{4,8},{8,12},{12,14},{14,10},{10,6},{6,2},{2,0},{0,4},{5,9},{9,13}... | collective-permute-start | bytes 786440 | tf_op jit(solution)/shard_map/ppermute | solution.py:172
  110.4 38.4 %collective-permute-start.15 = (bf16[128,1024]{0,1:T(8,128)(2,1)S(1)}, bf16[128,1024]{0,1:T(8,128)(2,1)}, u32[]{:S(2)}, u32[]{:S(2)}) collective-permute-start(bf16[128,1024]{0,1:T(8,128)(2,1)S(1)} %convert_bitcast_fusion), channel_id=1, source_target_pairs={{8,4},{12,8},{14,12},{10,14},{6,10},{2,6},{0,2},{4,0},{9,5},{13,9}... | collective-permute-start | bytes 786440 | tf_op jit(solution)/shard_map/ppermute | solution.py:175
  110.4 1.4 collective-permute-start.21
  113.3 25.9 %copy-start.11 = (pred[8]{0:T(512)(128)(4,1)S(1)}, pred[8]{0:T(512)(128)(4,1)}, u32[]{:S(2)}) copy-start(pred[8]{0:T(512)(128)(4,1)} %copy-done.9) | copy-start | bytes 28
  113.3 7.0 %collective-permute-start.22 = (f32[128,128]{1,0:T(8,128)S(1)}, f32[128,128]{1,0:T(8,128)S(1)}, u32[]{:S(2)}, u32[]{:S(2)}) collective-permute-start(f32[128,128]{1,0:T(8,128)S(1)} %get-tuple-element.3), channel_id=1, source_target_pairs={{0,2},{2,4},{4,6},{6,8},{8,10},{10,12},{12,14},{14,0},{1,3},{3,5},... | collective-permute-start | bytes 196616 | tf_op jit(solution)/shard_map/ppermute | solution.py:111
  117.2 6.3 %collective-permute-start.23 = (f32[128,128]{1,0:T(8,128)S(1)}, f32[128,128]{1,0:T(8,128)S(1)}, u32[]{:S(2)}, u32[]{:S(2)}) collective-permute-start(f32[128,128]{1,0:T(8,128)S(1)} %get-tuple-element.3), channel_id=1, source_target_pairs={{0,4},{2,6},{4,8},{6,10},{8,12},{10,14},{12,0},{14,2},{1,5},{3,7},... | collective-permute-start | bytes 196616 | tf_op jit(solution)/shard_map/ppermute | solution.py:111
  119.0 9.8 %collective-permute-start.24 = (f32[128,128]{1,0:T(8,128)S(1)}, f32[128,128]{1,0:T(8,128)S(1)}, u32[]{:S(2)}, u32[]{:S(2)}) collective-permute-start(f32[128,128]{1,0:T(8,128)S(1)} %get-tuple-element.3), channel_id=1, source_target_pairs={{0,6},{2,8},{4,10},{6,12},{8,14},{10,0},{12,2},{14,4},{1,7},{3,9},... | collective-permute-start | bytes 196616 | tf_op jit(solution)/shard_map/ppermute | solution.py:111
  120.2 12.4 %collective-permute-start.25 = (f32[128,128]{1,0:T(8,128)S(1)}, f32[128,128]{1,0:T(8,128)S(1)}, u32[]{:S(2)}, u32[]{:S(2)}) collective-permute-start(f32[128,128]{1,0:T(8,128)S(1)} %get-tuple-element.3), channel_id=1, source_target_pairs={{0,8},{2,10},{4,12},{6,14},{8,0},{10,2},{12,4},{14,6},{1,9},{3,11}... | collective-permute-start | bytes 196616 | tf_op jit(solution)/shard_map/ppermute | solution.py:111
  123.5 9.9 %collective-permute-start.26 = (f32[128,128]{1,0:T(8,128)S(1)}, f32[128,128]{1,0:T(8,128)S(1)}, u32[]{:S(2)}, u32[]{:S(2)}) collective-permute-start(f32[128,128]{1,0:T(8,128)S(1)} %get-tuple-element.3), channel_id=1, source_target_pairs={{0,10},{2,12},{4,14},{6,0},{8,2},{10,4},{12,6},{14,8},{1,11},{3,13... | collective-permute-start | bytes 196616 | tf_op jit(solution)/shard_map/ppermute | solution.py:111
  128.8 5.2 %collective-permute-start.27 = (f32[128,128]{1,0:T(8,128)S(1)}, f32[128,128]{1,0:T(8,128)S(1)}, u32[]{:S(2)}, u32[]{:S(2)}) collective-permute-start(f32[128,128]{1,0:T(8,128)S(1)} %get-tuple-element.3), channel_id=1, source_target_pairs={{0,12},{2,14},{4,0},{6,2},{8,4},{10,6},{12,8},{14,10},{1,13},{3,15... | collective-permute-start | bytes 196616 | tf_op jit(solution)/shard_map/ppermute | solution.py:111
  132.6 4.3 %collective-permute-start.28 = (f32[128,128]{1,0:T(8,128)S(1)}, f32[128,128]{1,0:T(8,128)S(1)}, u32[]{:S(2)}, u32[]{:S(2)}) collective-permute-start(f32[128,128]{1,0:T(8,128)S(1)} %get-tuple-element.3), channel_id=1, source_target_pairs={{0,14},{2,0},{4,2},{6,4},{8,6},{10,8},{12,10},{14,12},{1,15},{3,1}... | collective-permute-start | bytes 196616 | tf_op jit(solution)/shard_map/ppermute | solution.py:111
  142.6 4.8 %copy-start.7 = (f32[1024]{0:T(1024)S(1)}, f32[1024]{0:T(1024)}, u32[]{:S(2)}) copy-start(f32[1024]{0:T(1024)} %get-tuple-element.36) | copy-start | bytes 12292
  142.6 4.8 %copy-start.8 = (f32[1024]{0:T(1024)S(1)}, f32[1024]{0:T(1024)}, u32[]{:S(2)}) copy-start(f32[1024]{0:T(1024)} %get-tuple-element.37) | copy-start | bytes 12292
  143.7 5.1 %copy-start.5 = (f32[1024]{0:T(1024)S(1)}, f32[1024]{0:T(1024)}, u32[]{:S(2)}) copy-start(f32[1024]{0:T(1024)} %get-tuple-element.34) | copy-start | bytes 12292
  143.7 5.1 %copy-start.6 = (f32[1024]{0:T(1024)S(1)}, f32[1024]{0:T(1024)}, u32[]{:S(2)}) copy-start(f32[1024]{0:T(1024)} %get-tuple-element.35) | copy-start | bytes 12292
  147.4 7.7 %copy-start.3 = (f32[1024]{0:T(1024)S(1)}, f32[1024]{0:T(1024)}, u32[]{:S(2)}) copy-start(f32[1024]{0:T(1024)} %get-tuple-element.32) | copy-start | bytes 12292
  147.4 7.7 %copy-start.4 = (f32[1024]{0:T(1024)S(1)}, f32[1024]{0:T(1024)}, u32[]{:S(2)}) copy-start(f32[1024]{0:T(1024)} %get-tuple-element.33) | copy-start | bytes 12292
  147.4 7.7 %collective-permute-start.16 = (bf16[128,1024]{0,1:T(8,128)(2,1)}, bf16[128,1024]{0,1:T(8,128)(2,1)S(1)}, u32[]{:S(2)}, u32[]{:S(2)}) collective-permute-start(bf16[128,1024]{0,1:T(8,128)(2,1)} %collective-permute-done.14), channel_id=1, source_target_pairs={{4,8},{8,12},{12,14},{14,10},{10,6},{6,2},{2,0},{0,4},{5,9},{9,13}... | collective-permute-start | bytes 786440 | tf_op jit(solution)/shard_map/ppermute | solution.py:172
  150.4 6.6 %collective-permute-start.17 = (bf16[128,1024]{0,1:T(8,128)(2,1)}, bf16[128,1024]{0,1:T(8,128)(2,1)S(1)}, u32[]{:S(2)}, u32[]{:S(2)}) collective-permute-start(bf16[128,1024]{0,1:T(8,128)(2,1)} %collective-permute-done.15), channel_id=1, source_target_pairs={{8,4},{12,8},{14,12},{10,14},{6,10},{2,6},{0,2},{4,0},{9,5},{13,9}... | collective-permute-start | bytes 786440 | tf_op jit(solution)/shard_map/ppermute | solution.py:175
  155.1 8.1 %collective-permute-start.18 = (bf16[128,1024]{0,1:T(8,128)(2,1)S(1)}, bf16[128,1024]{0,1:T(8,128)(2,1)S(1)}, u32[]{:S(2)}, u32[]{:S(2)}) collective-permute-start(bf16[128,1024]{0,1:T(8,128)(2,1)S(1)} %collective-permute-done.16), channel_id=1, source_target_pairs={{4,8},{8,12},{12,14},{14,10},{10,6},{6,2},{2,0},{0,4},{5,9},{9,13}... | collective-permute-start | bytes 786440 | tf_op jit(solution)/shard_map/ppermute | solution.py:172
  157.1 0.7 copy-start.12
  158.4 6.6 %collective-permute-start.19 = (bf16[128,1024]{0,1:T(8,128)(2,1)}, bf16[128,1024]{0,1:T(8,128)(2,1)S(1)}, u32[]{:S(2)}, u32[]{:S(2)}) collective-permute-start(bf16[128,1024]{0,1:T(8,128)(2,1)} %copy-done.12), channel_id=1, source_target_pairs={{8,4},{12,8},{14,12},{10,14},{6,10},{2,6},{0,2},{4,0},{9,5},{13,9}... | collective-permute-start | bytes 786440 | tf_op jit(solution)/shard_map/ppermute | solution.py:175
  163.2 6.4 %collective-permute-start.20 = (bf16[128,1024]{0,1:T(8,128)(2,1)S(1)}, bf16[128,1024]{0,1:T(8,128)(2,1)S(1)}, u32[]{:S(2)}, u32[]{:S(2)}) collective-permute-start(bf16[128,1024]{0,1:T(8,128)(2,1)S(1)} %collective-permute-done.18), channel_id=1, source_target_pairs={{4,8},{8,12},{12,14},{14,10},{10,6},{6,2},{2,0},{0,4},{5,9},{9,13}... | collective-permute-start | bytes 786440 | tf_op jit(solution)/shard_map/ppermute | solution.py:172
